TPU v7x, 512 devices: a whole 4x8x8 slice. The times are simulated.
512 devices in a mesh: gx: 32 (over x, y), gy: 16 (over z, core).
Axes of the slice: x: 4, y: 8, z: 8, core: 2. Of those that a mesh axis runs over, the one named last changes fastest.
Arguments:
- test_block: float32 [32, 8, 512, 2048], P(None, None, 'gx', 'gy'), may hold values from -1500 to 1500, as said below
- kappa_sq: float32 [8, 512, 2048], P(None, 'gx', 'gy'), may hold values from 0.05 to 2
Outputs:
- basis: float32 [32, 8, 512, 2048], P(None, None, 'gx', 'gy')
Inputs may be any that keep to these rules, and one draw needn't show every extreme that they name: `test_block`: real-valued entries.
All inputs are finite; a program needn't handle non-finite values.
Results may differ from a plain program's by a relative error of at most 0.0003.
Values sent between devices are 32-bit elements; how exact they have to be, the bound alone decides.
No kernel may reach another device: no remote copies, remote signals or barrier semaphores. Data moves between devices by JAX's collectives and lax.ppermute only.
A program may use at most 64 MiB of HBM per device.

v0:
```python
import math
import jax
import jax.numpy as jnp
from jax import lax
from jax.sharding import PartitionSpec as P


def extended(block, sides, width):
    for axis, dim in sides:
        count = lax.axis_size(axis)
        forward = [(i, i + 1) for i in range(count - 1)]
        backward = [(target, source) for source, target in forward]
        low = lax.ppermute(
            lax.slice_in_dim(block, block.shape[dim] - width, None, axis=dim), axis, forward
        )
        high = lax.ppermute(lax.slice_in_dim(block, 0, width, axis=dim), axis, backward)
        block = jnp.concatenate([low, block, high], axis=dim)
    return block


def stencil(padded, coefficient):
    center = padded[:, :, 1:-1, 1:-1]
    neighbours = padded[:, :, 2:, 1:-1] + padded[:, :, :-2, 1:-1]
    neighbours = neighbours + padded[:, :, 1:-1, 2:] + padded[:, :, 1:-1, :-2]
    z_padded = jnp.pad(center, ((0, 0), (1, 1), (0, 0), (0, 0)))
    neighbours = neighbours + z_padded[:, 2:] + z_padded[:, :-2]
    return (6.0 + coefficient) * center - neighbours


def lower_solve(factor, block):
    return lax.linalg.triangular_solve(factor, block, left_side=True, lower=True)


def apply_once(field_in, kappa_sq):
    padded = extended(field_in, (("gx", 2), ("gy", 3)), 1)
    return stencil(padded, kappa_sq)


def merge_factors(stacked):
    summed = jnp.einsum("nij,nkj->ik", stacked, stacked, precision=lax.Precision.HIGHEST)
    return jnp.linalg.cholesky(summed)


def merged_factor(gram_matrix):
    stacked = lax.all_gather(gram_matrix[None], "gx", axis=0, tiled=True)
    column_factor = jnp.linalg.cholesky(jnp.sum(stacked, axis=0))
    stacked_columns = lax.all_gather(column_factor[None], "gy", axis=0, tiled=True)
    return merge_factors(stacked_columns)


def body(test_block, kappa_sq):
    cols_here, depth_here, x_cells, y_cells = test_block.shape
    sample = apply_once(apply_once(test_block, kappa_sq), kappa_sq)
    flattened = sample.reshape(cols_here, -1)
    gram_one = jnp.dot(flattened, flattened.T, precision=lax.Precision.HIGHEST)
    factor_one = merged_factor(gram_one)
    partial_value = lower_solve(factor_one, flattened)
    gram_two = jnp.dot(partial_value, partial_value.T, precision=lax.Precision.HIGHEST)
    factor_two = merged_factor(gram_two)
    scale_factor = math.sqrt(flattened.shape[1] * lax.axis_size("gx") * lax.axis_size("gy"))
    result = lower_solve(factor_two, partial_value) * scale_factor
    return result.reshape(cols_here, depth_here, x_cells, y_cells)


def solution(mesh):
    in_specs = (P(None, None, "gx", "gy"), P(None, "gx", "gy"))
    out_specs = P(None, None, "gx", "gy")
    return jax.shard_map(body, mesh=mesh, in_specs=in_specs, out_specs=out_specs, check_vma=False)
```

profile of v0, /device:TPU:1, one launch (start us, length us, event | category | flops | bytes accessed | tf_op | source)
XLA Modules:
  0.0 260.5 jit_solution(14732550015322631781)
XLA Ops:
  0.0 2.6 %copy.82 = f32[32,8,16,128]{3,1,2,0:T(8,128)S(1)} copy(f32[32,8,16,128]{3,2,1,0:T(8,128)} %param.5) | data formatting | bytes 4194304 | tf_op args[0]
  4.0 4.0 %collective-permute-start.1 = (f32[32,8,1,128]{3,1,2,0:T(8,128)S(1)}, f32[32,8,1,128]{3,1,2,0:T(8,128)S(1)}, u32[]{:S(2)}, u32[]{:S(2)}) collective-permute-start(f32[32,8,1,128]{3,1,2,0:T(8,128)S(1)} %get-tuple-element.13), channel_id=1, source_target_pairs={{0,16},{16,32},{32,48},{48,64},{64,80},{80,96},{96,112},{112,128},... | collective-permute-start | bytes 393224 | tf_op jit(solution)/shard_map/ppermute | solution.py:13
  9.3 4.5 %copy.88 = f32[32,8,16,128]{0,1,3,2:T(8,128)} copy(f32[32,8,16,128]{3,2,1,0:T(8,128)S(1)} %copy-done.2) | data formatting | bytes 4194304 | tf_op args[0]
  14.4 3.9 %pad_maximum_fusion = f32[32,8,18,128]{0,1,3,2:T(8,128)S(1)} fusion(f32[32,8,1,128]{0,1,3,2:T(8,128)S(1)} %copy.89, f32[32,8,16,128]{0,1,3,2:T(8,128)} %copy.88, f32[32,8,1,128]{0,1,3,2:T(8,128)S(1)} %copy.87), kind=kLoop, calls=%fused_computation.1 | loop fusion | flops 1179648 | bytes 4718592 | tf_op jit(solution)/shard_map/concatenate | solution.py:17
  18.4 3.6 %copy-done = f32[32,8,18,128]{0,1,3,2:T(8,128)} copy-done((f32[32,8,18,128]{0,1,3,2:T(8,128)}, f32[32,8,18,128]{0,1,3,2:T(8,128)S(1)}, u32[]{:S(2)}) %copy-start) | copy-done | bytes 2359320
  22.0 6.8 %collective-permute-start.2 = (f32[32,8,18,1]{0,1,3,2:T(8,128)S(1)}, f32[32,8,18,1]{0,1,3,2:T(8,128)S(1)}, u32[]{:S(2)}, u32[]{:S(2)}) collective-permute-start(f32[32,8,18,1]{0,1,3,2:T(8,128)S(1)} %get-tuple-element.6), channel_id=1, source_target_pairs={{1,0},{2,1},{3,2},{4,3},{5,4},{6,5},{7,6},{8,7},{9,8},{10,9},{11,1... | collective-permute-start | bytes 55304 | tf_op jit(solution)/shard_map/ppermute | solution.py:16
  30.7 7.9 %copy.90 = f32[32,8,18,128]{3,1,2,0:T(8,128)} copy(f32[32,8,18,128]{0,1,3,2:T(8,128)} %copy-done) | data formatting | bytes 4718592 | tf_op jit(solution)/shard_map/concatenate | solution.py:17
  43.3 8.0 %fusion.2 = f32[32,8,16,128]{3,1,2,0:T(8,128)S(1)} fusion(f32[32,8,16,128]{3,1,2,0:T(8,128)} %copy-done.1, f32[32,8,18,128]{3,1,2,0:T(8,128)} %copy.90, f32[32,8,18,1]{3,1,2,0:T(8,128)} %copy.92, f32[32,8,18,1]{3,1,2,0:T(8,128)} %copy.91, f32[32,8,1,128]{3,1,2,0:T(8,128)S(1)} %collective-permute-done.1, f32[32,8,1,128]{3,1,2,0:T(8,128)S(1)} %collective-permute-done, ...), kind=kLoop, calls=%fused_computation.9 | loop fusion | flops 5767168 | bytes 6918144 | tf_op jit(solution)/shard_map/sub | solution.py:27
  52.7 4.2 %collective-permute-start.5 = (f32[32,8,1,128]{3,1,2,0:T(8,128)S(1)}, f32[32,8,1,128]{3,1,2,0:T(8,128)S(1)}, u32[]{:S(2)}, u32[]{:S(2)}) collective-permute-start(f32[32,8,1,128]{3,1,2,0:T(8,128)S(1)} %get-tuple-element.11), channel_id=1, source_target_pairs={{0,16},{16,32},{32,48},{48,64},{64,80},{80,96},{96,112},{112,128},... | collective-permute-start | bytes 393224 | tf_op jit(solution)/shard_map/ppermute | solution.py:13
  59.2 2.9 %fusion.38 = (f32[32,8,18,1]{3,1,2,0:T(8,128)}, f32[32,8,18,1]{3,1,2,0:T(8,128)}) fusion(f32[32,8,18,128]{3,1,2,0:T(8,128)S(1)} %pad_maximum_fusion.1), kind=kLoop, calls=%fused_computation.71 | loop fusion | bytes 73728 | tf_op jit(solution)/shard_map/slice | solution.py:16
  62.1 2.6 copy.107
  64.7 3.4 %collective-permute-start.6 = (f32[32,8,18,1]{0,1,3,2:T(8,128)S(1)}, f32[32,8,18,1]{0,1,3,2:T(8,128)S(1)}, u32[]{:S(2)}, u32[]{:S(2)}) collective-permute-start(f32[32,8,18,1]{0,1,3,2:T(8,128)S(1)} %copy.107), channel_id=1, source_target_pairs={{1,0},{2,1},{3,2},{4,3},{5,4},{6,5},{7,6},{8,7},{9,8},{10,9},{11,1... | collective-permute-start | bytes 55304 | tf_op jit(solution)/shard_map/ppermute | solution.py:16
  68.1 2.6 copy.108
  77.7 4.0 %fusion.5 = f32[32,8,16,128]{3,1,2,0:T(8,128)S(1)} fusion(f32[32,8,16,128]{3,1,2,0:T(8,128)S(1)} %fusion.2, f32[32,8,18,1]{3,1,2,0:T(8,128)} %copy.98, f32[32,8,1,128]{3,1,2,0:T(8,128)S(1)} %collective-permute-done.4, f32[32,8,1,128]{3,1,2,0:T(8,128)S(1)} %collective-permute-done.5, f32[32,8,18,1]{3,1,2,0:T(8,128)} %copy.96, f32[8,16,128]{2,0,1:T(8,128)S(1)} %copy.81), kind=kLoop, calls=%fused_computation.12 | loop fusion | flops 7864320 | bytes 4558848 | tf_op jit(solution)/shard_map/sub | solution.py:27
  81.8 2.8 %fusion.18 = f32[32,32]{1,0:T(8,128)S(1)} fusion(f32[32,8,16,128]{3,1,2,0:T(8,128)S(1)} %fusion.5), kind=kOutput, calls=%fused_computation.37 | convolution fusion | flops 201326592 | bytes 2101248 | tf_op jit(solution)/shard_map/dot_general | solution.py:55
  86.3 43.5 %all-gather = f32[1024,32]{1,0:T(8,128)S(1)} all-gather(f32[32,32]{1,0:T(8,128)S(1)} %fusion.18), channel_id=2, replica_groups=mesh['gx'=32,'gy'=16] {'gx'}, dimensions={0}, use_global_device_ids=true | all-gather | bytes 135168 | tf_op jit(solution)/shard_map/all_gather | solution.py:45
  130.0 2.9 %cholesky.74 = f32[32,32]{1,0:T(8,128)S(1)} custom-call(f32[32,32]{1,0:T(8,128)S(1)} %fusion.28), custom_call_target="Cholesky" | custom-call | tf_op jit(solution)/shard_map/jit(cholesky)/cholesky | solution.py:46
  134.3 35.5 %all-gather.1 = f32[512,32]{1,0:T(8,128)S(1)} all-gather(f32[32,32]{1,0:T(8,128)S(1)} %fusion.30), channel_id=3, replica_groups=mesh['gx'=32,'gy'=16] {'gy'}, dimensions={0}, use_global_device_ids=true | all-gather | bytes 69632 | tf_op jit(solution)/shard_map/all_gather | solution.py:47
  170.2 2.9 %cholesky.85 = f32[32,32]{1,0:T(8,128)S(1)} custom-call(f32[32,32]{1,0:T(8,128)S(1)} %fusion.27), custom_call_target="Cholesky" | custom-call | tf_op jit(solution)/shard_map/jit(cholesky)/cholesky | solution.py:41
  177.0 4.6 %fusion.6 = f32[32,16384]{1,0:T(8,128)S(1)} fusion(f32[4,8,128,128]{3,2,1,0:T(8,128)} %bitcast.54, f32[1,32,32]{1,2,0:T(8,128)S(1)} %custom-call.6), kind=kOutput, calls=%fused_computation.13 | convolution fusion | flops 201326592 | bytes 4198400 | tf_op jit(solution)/shard_map/triangular_solve/dot.1 | solution.py:31
  183.4 35.5 %all-gather.2 = f32[1024,32]{1,0:T(8,128)S(1)} all-gather(f32[32,32]{1,0:T(8,128)S(1)} %fusion.41), channel_id=4, replica_groups=mesh['gx'=32,'gy'=16] {'gx'}, dimensions={0}, use_global_device_ids=true | all-gather | bytes 135168 | tf_op jit(solution)/shard_map/all_gather | solution.py:45
  219.1 2.9 %cholesky.96 = f32[32,32]{1,0:T(8,128)S(1)} custom-call(f32[32,32]{1,0:T(8,128)S(1)} %fusion.25), custom_call_target="Cholesky" | custom-call | tf_op jit(solution)/shard_map/jit(cholesky)/cholesky | solution.py:46
  223.3 26.4 %all-gather.3 = f32[512,32]{1,0:T(8,128)S(1)} all-gather(f32[32,32]{1,0:T(8,128)S(1)} %fusion.29), channel_id=5, replica_groups=mesh['gx'=32,'gy'=16] {'gy'}, dimensions={0}, use_global_device_ids=true | all-gather | bytes 69632 | tf_op jit(solution)/shard_map/all_gather | solution.py:47
  250.2 2.9 %cholesky.107 = f32[32,32]{1,0:T(8,128)S(1)} custom-call(f32[32,32]{1,0:T(8,128)S(1)} %fusion.24), custom_call_target="Cholesky" | custom-call | tf_op jit(solution)/shard_map/jit(cholesky)/cholesky | solution.py:41
  (61 shorter events, 39.1 us)
Async XLA Ops:
  0.0 9.3 %copy-start.2 = (f32[32,8,16,128]{3,2,1,0:T(8,128)S(1)}, f32[32,8,16,128]{3,2,1,0:T(8,128)}, u32[]{:S(2)}) copy-start(f32[32,8,16,128]{3,2,1,0:T(8,128)} %param.5) | copy-start | bytes 6291460
  2.6 1.3 copy-start.1
  4.0 9.9 %collective-permute-start.1 = (f32[32,8,1,128]{3,1,2,0:T(8,128)S(1)}, f32[32,8,1,128]{3,1,2,0:T(8,128)S(1)}, u32[]{:S(2)}, u32[]{:S(2)}) collective-permute-start(f32[32,8,1,128]{3,1,2,0:T(8,128)S(1)} %get-tuple-element.13), channel_id=1, source_target_pairs={{0,16},{16,32},{32,48},{48,64},{64,80},{80,96},{96,112},{112,128},... | collective-permute-start | bytes 393224 | tf_op jit(solution)/shard_map/ppermute | solution.py:13
  8.0 6.1 %collective-permute-start = (f32[32,8,1,128]{3,1,2,0:T(8,128)S(1)}, f32[32,8,1,128]{3,1,2,0:T(8,128)S(1)}, u32[]{:S(2)}, u32[]{:S(2)}) collective-permute-start(f32[32,8,1,128]{3,1,2,0:T(8,128)S(1)} %get-tuple-element.14), channel_id=1, source_target_pairs={{16,0},{32,16},{48,32},{64,48},{80,64},{96,80},{112,96},{128,112},... | collective-permute-start | bytes 393224 | tf_op jit(solution)/shard_map/ppermute | solution.py:16
  14.4 16.3 %copy-start.3 = (f32[8,16,128]{2,1,0:T(8,128)S(1)}, f32[8,16,128]{2,1,0:T(8,128)}, u32[]{:S(2)}) copy-start(f32[8,16,128]{2,1,0:T(8,128)} %param.6) | copy-start | bytes 196612
  18.3 3.6 %copy-start = (f32[32,8,18,128]{0,1,3,2:T(8,128)}, f32[32,8,18,128]{0,1,3,2:T(8,128)S(1)}, u32[]{:S(2)}) copy-start(f32[32,8,18,128]{0,1,3,2:T(8,128)S(1)} %pad_maximum_fusion) | copy-start | bytes 7077892
  22.0 16.7 %collective-permute-start.2 = (f32[32,8,18,1]{0,1,3,2:T(8,128)S(1)}, f32[32,8,18,1]{0,1,3,2:T(8,128)S(1)}, u32[]{:S(2)}, u32[]{:S(2)}) collective-permute-start(f32[32,8,18,1]{0,1,3,2:T(8,128)S(1)} %get-tuple-element.6), channel_id=1, source_target_pairs={{1,0},{2,1},{3,2},{4,3},{5,4},{6,5},{7,6},{8,7},{9,8},{10,9},{11,1... | collective-permute-start | bytes 55304 | tf_op jit(solution)/shard_map/ppermute | solution.py:16
  28.7 12.3 %collective-permute-start.3 = (f32[32,8,18,1]{0,1,3,2:T(8,128)S(1)}, f32[32,8,18,1]{0,1,3,2:T(8,128)S(1)}, u32[]{:S(2)}, u32[]{:S(2)}) collective-permute-start(f32[32,8,18,1]{0,1,3,2:T(8,128)S(1)} %get-tuple-element.8), channel_id=1, source_target_pairs={{0,1},{1,2},{2,3},{3,4},{4,5},{5,6},{6,7},{7,8},{8,9},{9,10},{10,1... | collective-permute-start | bytes 55304 | tf_op jit(solution)/shard_map/ppermute | solution.py:13
  51.4 6.8 %collective-permute-start.4 = (f32[32,8,1,128]{3,1,2,0:T(8,128)S(1)}, f32[32,8,1,128]{3,1,2,0:T(8,128)S(1)}, u32[]{:S(2)}, u32[]{:S(2)}) collective-permute-start(f32[32,8,1,128]{3,1,2,0:T(8,128)S(1)} %get-tuple-element.12), channel_id=1, source_target_pairs={{16,0},{32,16},{48,32},{64,48},{80,64},{96,80},{112,96},{128,112},... | collective-permute-start | bytes 393224 | tf_op jit(solution)/shard_map/ppermute | solution.py:16
  52.7 6.4 %collective-permute-start.5 = (f32[32,8,1,128]{3,1,2,0:T(8,128)S(1)}, f32[32,8,1,128]{3,1,2,0:T(8,128)S(1)}, u32[]{:S(2)}, u32[]{:S(2)}) collective-permute-start(f32[32,8,1,128]{3,1,2,0:T(8,128)S(1)} %get-tuple-element.11), channel_id=1, source_target_pairs={{0,16},{16,32},{32,48},{48,64},{64,80},{80,96},{96,112},{112,128},... | collective-permute-start | bytes 393224 | tf_op jit(solution)/shard_map/ppermute | solution.py:13
  64.7 8.3 %collective-permute-start.6 = (f32[32,8,18,1]{0,1,3,2:T(8,128)S(1)}, f32[32,8,18,1]{0,1,3,2:T(8,128)S(1)}, u32[]{:S(2)}, u32[]{:S(2)}) collective-permute-start(f32[32,8,18,1]{0,1,3,2:T(8,128)S(1)} %copy.107), channel_id=1, source_target_pairs={{1,0},{2,1},{3,2},{4,3},{5,4},{6,5},{7,6},{8,7},{9,8},{10,9},{11,1... | collective-permute-start | bytes 55304 | tf_op jit(solution)/shard_map/ppermute | solution.py:16
  70.7 4.7 %collective-permute-start.7 = (f32[32,8,18,1]{0,1,3,2:T(8,128)S(1)}, f32[32,8,18,1]{0,1,3,2:T(8,128)S(1)}, u32[]{:S(2)}, u32[]{:S(2)}) collective-permute-start(f32[32,8,18,1]{0,1,3,2:T(8,128)S(1)} %copy.108), channel_id=1, source_target_pairs={{0,1},{1,2},{2,3},{3,4},{4,5},{5,6},{6,7},{7,8},{8,9},{9,10},{10,1... | collective-permute-start | bytes 55304 | tf_op jit(solution)/shard_map/ppermute | solution.py:13
where the time goes:
time: 261 us
  blocking collectives  141 us (54%)
  local copies, waits for them, and re-layouts  41.7 us (16%)
  other arithmetic  38.4 us (15%)
  starting transfers between devices  25.2 us (10%)
  matrix products  11.8 us (5%)
    all_gather x2, blocking collectives, merged_factor(): stacked = lax.all_gather(gram_matrix[None], 'gx', axis=0, tiled=True)  79 us
    all_gather x2, blocking collectives, merged_factor(): lax.all_gather(column_factor[None], 'gy', axis=0, tiled=True)  61.9 us
    unnamed x13, local copies, waits for them, and re-layouts  19 us
    ppermute x4, starting transfers between devices, extended(): lax.ppermute(lax.slice_in_dim(block, 0, width, axis=dim), axis, backward)  12.7 us
    ppermute x4, starting transfers between devices, extended(): lax.ppermute(lax.slice_in_dim(block, block.shape[dim] - width, None, axis...  12.5 us
    sub x2, other arithmetic, stencil(): return (6.0 + coefficient) * center - neighbours  12 us
    concatenate x1, local copies, waits for them, and re-layouts, extended(): block = jnp.concatenate([low, block, high], axis=dim)  7.95 us
    another operation x6, other arithmetic, merged_factor(): column_factor = jnp.linalg.cholesky(jnp.sum(stacked, axis=0))  7.27 us
  transfers between devices with their start and end apart: 8, of which 2 were waited for; matrix products, arithmetic and copies ran while one was open for 8% of the time, Pallas kernels for 0%

commit v1 on v0

--- a/solution.py
+++ b/solution.py
@@ -42,7 +42,9 @@
 
 
 def merged_factor(gram_matrix):
-    stacked = lax.all_gather(gram_matrix[None], "gx", axis=0, tiled=True)
+    stacked = jnp.concatenate(
+        lax.all_to_all(jnp.stack([gram_matrix[None]] * lax.axis_size("gx")), "gx", 0, 0), axis=0
+    )
     column_factor = jnp.linalg.cholesky(jnp.sum(stacked, axis=0))
     stacked_columns = lax.all_gather(column_factor[None], "gy", axis=0, tiled=True)
     return merge_factors(stacked_columns)

time: 261 us -> 200 us (0.77)
  blocking collectives: 141 us -> 53.6 us
  starting transfers between devices: 25.2 us -> 38.2 us
  waiting for transfers between devices: 2.24 us -> 8.95 us
  local copies, waits for them, and re-layouts: 41.7 us -> 46.7 us
    all_gather x2 -> x0, blocking collectives: 79 us -> none  [merged_factor(): stacked = lax.all_gather(gram_matrix[None], 'gx', axis=0, tiled=True)]
    all_gather x2, blocking collectives: 61.9 us -> 41.2 us  [merged_factor(): lax.all_gather(column_factor[None], 'gy', axis=0, tiled=True)]
    all_to_all x0 -> x1, starting transfers between devices: none -> 13.1 us  [merged_factor(): lax.all_to_all(jnp.stack([gram_matrix[None]] * lax.axis_size('gx')), 'gx'...]
    all_to_all x0 -> x1, blocking collectives: none -> 12.4 us  [merged_factor(): lax.all_to_all(jnp.stack([gram_matrix[None]] * lax.axis_size('gx')), 'gx'...]
    all_to_all x0 -> x1, waiting for transfers between devices: none -> 6.71 us  [merged_factor(): lax.all_to_all(jnp.stack([gram_matrix[None]] * lax.axis_size('gx')), 'gx'...]
    unnamed x13 -> x19, local copies, waits for them, and re-layouts: 19 us -> 21.8 us
  transfers between devices with their start and end apart: 8 -> 9, of which waited for: 2 -> 3; matrix products, arithmetic and copies ran while one was open for 8% -> 12% of each run, Pallas kernels for 0% -> 0%
where the time goes in v1:
time: 200 us
  blocking collectives  53.6 us (27%)
  local copies, waits for them, and re-layouts  46.7 us (23%)
  other arithmetic  40 us (20%)
  starting transfers between devices  38.2 us (19%)
  matrix products  11.8 us (6%)
  waiting for transfers between devices  8.95 us (4%)
    all_gather x2, blocking collectives, merged_factor(): lax.all_gather(column_factor[None], 'gy', axis=0, tiled=True)  41.2 us
    unnamed x19, local copies, waits for them, and re-layouts  21.8 us
    all_to_all x1, starting transfers between devices, merged_factor(): lax.all_to_all(jnp.stack([gram_matrix[None]] * lax.axis_size('gx')), 'gx'...  13.1 us
    ppermute x4, starting transfers between devices, extended(): lax.ppermute(lax.slice_in_dim(block, 0, width, axis=dim), axis, backward)  12.7 us
    ppermute x4, starting transfers between devices, extended(): lax.ppermute(lax.slice_in_dim(block, block.shape[dim] - width, None, axis...  12.5 us
    all_to_all x1, blocking collectives, merged_factor(): lax.all_to_all(jnp.stack([gram_matrix[None]] * lax.axis_size('gx')), 'gx'...  12.4 us
    sub x2, other arithmetic, stencil(): return (6.0 + coefficient) * center - neighbours  12 us
    concatenate x1, local copies, waits for them, and re-layouts, extended(): block = jnp.concatenate([low, block, high], axis=dim)  7.95 us
  transfers between devices with their start and end apart: 9, of which 3 were waited for; matrix products, arithmetic and copies ran while one was open for 12% of the time, Pallas kernels for 0%

profile of v1, /device:TPU:1, one launch (start us, length us, event | category | flops | bytes accessed | tf_op | source)
XLA Modules:
  0.0 199.7 jit_solution(16346007854412705644)
XLA Ops:
  0.0 2.6 %copy.82 = f32[32,8,16,128]{3,1,2,0:T(8,128)S(1)} copy(f32[32,8,16,128]{3,2,1,0:T(8,128)} %param.5) | data formatting | bytes 4194304 | tf_op args[0]
  4.0 4.0 %collective-permute-start.1 = (f32[32,8,1,128]{3,1,2,0:T(8,128)S(1)}, f32[32,8,1,128]{3,1,2,0:T(8,128)S(1)}, u32[]{:S(2)}, u32[]{:S(2)}) collective-permute-start(f32[32,8,1,128]{3,1,2,0:T(8,128)S(1)} %get-tuple-element.13), channel_id=1, source_target_pairs={{0,16},{16,32},{32,48},{48,64},{64,80},{80,96},{96,112},{112,128},... | collective-permute-start | bytes 393224 | tf_op jit(solution)/shard_map/ppermute | solution.py:13
  9.3 4.5 %copy.88 = f32[32,8,16,128]{0,1,3,2:T(8,128)} copy(f32[32,8,16,128]{3,2,1,0:T(8,128)S(1)} %copy-done.3) | data formatting | bytes 4194304 | tf_op args[0]
  14.4 3.9 %pad_maximum_fusion = f32[32,8,18,128]{0,1,3,2:T(8,128)S(1)} fusion(f32[32,8,1,128]{0,1,3,2:T(8,128)S(1)} %copy.89, f32[32,8,16,128]{0,1,3,2:T(8,128)} %copy.88, f32[32,8,1,128]{0,1,3,2:T(8,128)S(1)} %copy.87), kind=kLoop, calls=%fused_computation.1 | loop fusion | flops 1179648 | bytes 4718592 | tf_op jit(solution)/shard_map/concatenate | solution.py:17
  18.4 3.6 %copy-done = f32[32,8,18,128]{0,1,3,2:T(8,128)} copy-done((f32[32,8,18,128]{0,1,3,2:T(8,128)}, f32[32,8,18,128]{0,1,3,2:T(8,128)S(1)}, u32[]{:S(2)}) %copy-start) | copy-done | bytes 2359320
  22.0 6.8 %collective-permute-start.2 = (f32[32,8,18,1]{0,1,3,2:T(8,128)S(1)}, f32[32,8,18,1]{0,1,3,2:T(8,128)S(1)}, u32[]{:S(2)}, u32[]{:S(2)}) collective-permute-start(f32[32,8,18,1]{0,1,3,2:T(8,128)S(1)} %get-tuple-element.6), channel_id=1, source_target_pairs={{1,0},{2,1},{3,2},{4,3},{5,4},{6,5},{7,6},{8,7},{9,8},{10,9},{11,1... | collective-permute-start | bytes 55304 | tf_op jit(solution)/shard_map/ppermute | solution.py:16
  30.7 7.9 %copy.90 = f32[32,8,18,128]{3,1,2,0:T(8,128)} copy(f32[32,8,18,128]{0,1,3,2:T(8,128)} %copy-done) | data formatting | bytes 4718592 | tf_op jit(solution)/shard_map/concatenate | solution.py:17
  43.3 8.0 %fusion.2 = f32[32,8,16,128]{3,1,2,0:T(8,128)S(1)} fusion(f32[32,8,16,128]{3,1,2,0:T(8,128)} %copy-done.2, f32[32,8,18,128]{3,1,2,0:T(8,128)} %copy.90, f32[32,8,18,1]{3,1,2,0:T(8,128)} %copy.92, f32[32,8,18,1]{3,1,2,0:T(8,128)} %copy.91, f32[32,8,1,128]{3,1,2,0:T(8,128)S(1)} %collective-permute-done.1, f32[32,8,1,128]{3,1,2,0:T(8,128)S(1)} %collective-permute-done, ...), kind=kLoop, calls=%fused_computation.9 | loop fusion | flops 5767168 | bytes 6918144 | tf_op jit(solution)/shard_map/sub | solution.py:27
  52.7 4.2 %collective-permute-start.5 = (f32[32,8,1,128]{3,1,2,0:T(8,128)S(1)}, f32[32,8,1,128]{3,1,2,0:T(8,128)S(1)}, u32[]{:S(2)}, u32[]{:S(2)}) collective-permute-start(f32[32,8,1,128]{3,1,2,0:T(8,128)S(1)} %get-tuple-element.11), channel_id=1, source_target_pairs={{0,16},{16,32},{32,48},{48,64},{64,80},{80,96},{96,112},{112,128},... | collective-permute-start | bytes 393224 | tf_op jit(solution)/shard_map/ppermute | solution.py:13
  59.2 2.9 %fusion.38 = (f32[32,8,18,1]{3,1,2,0:T(8,128)}, f32[32,8,18,1]{3,1,2,0:T(8,128)}) fusion(f32[32,8,18,128]{3,1,2,0:T(8,128)S(1)} %pad_maximum_fusion.1), kind=kLoop, calls=%fused_computation.71 | loop fusion | bytes 73728 | tf_op jit(solution)/shard_map/slice | solution.py:16
  64.7 3.4 %collective-permute-start.6 = (f32[32,8,18,1]{0,1,3,2:T(8,128)S(1)}, f32[32,8,18,1]{0,1,3,2:T(8,128)S(1)}, u32[]{:S(2)}, u32[]{:S(2)}) collective-permute-start(f32[32,8,18,1]{0,1,3,2:T(8,128)S(1)} %copy.107), channel_id=1, source_target_pairs={{1,0},{2,1},{3,2},{4,3},{5,4},{6,5},{7,6},{8,7},{9,8},{10,9},{11,1... | collective-permute-start | bytes 55304 | tf_op jit(solution)/shard_map/ppermute | solution.py:16
  77.7 4.0 %fusion.5 = f32[32,8,16,128]{3,1,2,0:T(8,128)S(1)} fusion(f32[32,8,16,128]{3,1,2,0:T(8,128)S(1)} %fusion.2, f32[32,8,18,1]{3,1,2,0:T(8,128)} %copy.98, f32[32,8,1,128]{3,1,2,0:T(8,128)S(1)} %collective-permute-done.4, f32[32,8,1,128]{3,1,2,0:T(8,128)S(1)} %collective-permute-done.5, f32[32,8,18,1]{3,1,2,0:T(8,128)} %copy.96, f32[8,16,128]{2,0,1:T(8,128)S(1)} %copy.81), kind=kLoop, calls=%fused_computation.12 | loop fusion | flops 7864320 | bytes 4558848 | tf_op jit(solution)/shard_map/sub | solution.py:27
  83.1 2.8 %fusion.18 = f32[32,32]{1,0:T(8,128)S(1)} fusion(f32[32,8,16,128]{3,1,2,0:T(8,128)S(1)} %fusion.5), kind=kOutput, calls=%fused_computation.37 | convolution fusion | flops 201326592 | bytes 2101248 | tf_op jit(solution)/shard_map/dot_general | solution.py:57
  86.9 13.1 %all-to-all-start = ((f32[32,1,1024]{2,1,0:T(1,128)}), f32[32,1,1024]{2,1,0:T(1,128)S(1)}, u32[]{:S(2)}, u32[]{:S(2)}) async-start(f32[32,1,1024]{2,1,0:T(1,128)} %reshape.37), calls=%async_computation | async-start | bytes 262144 | tf_op jit(solution)/shard_map/all_to_all | solution.py:46
  100.0 3.3 %copy.103 = f32[32,8,16,128]{3,2,1,0:T(8,128)} copy(f32[32,8,16,128]{3,1,2,0:T(8,128)} %copy-done.1) | data formatting | bytes 4194304 | tf_op jit(solution)/shard_map/sub | solution.py:27
  103.3 6.7 %all-to-all-done = f32[32,1,1024]{2,1,0:T(1,128)S(1)} async-done(((f32[32,1,1024]{2,1,0:T(1,128)}), f32[32,1,1024]{2,1,0:T(1,128)S(1)}, u32[]{:S(2)}, u32[]{:S(2)}) %all-to-all-start) | async-done | bytes 131104 | tf_op jit(solution)/shard_map/all_to_all | solution.py:46
  111.8 2.9 %cholesky.74 = f32[32,32]{1,0:T(8,128)S(1)} custom-call(f32[32,32]{1,0:T(8,128)S(1)} %fusion.28), custom_call_target="Cholesky" | custom-call | tf_op jit(solution)/shard_map/jit(cholesky)/cholesky | solution.py:48
  116.0 24.4 %all-gather = f32[512,32]{1,0:T(8,128)S(1)} all-gather(f32[32,32]{1,0:T(8,128)S(1)} %fusion.30), channel_id=2, replica_groups=mesh['gx'=32,'gy'=16] {'gy'}, dimensions={0}, use_global_device_ids=true | all-gather | bytes 69632 | tf_op jit(solution)/shard_map/all_gather | solution.py:49
  140.8 2.9 %cholesky.85 = f32[32,32]{1,0:T(8,128)S(1)} custom-call(f32[32,32]{1,0:T(8,128)S(1)} %fusion.27), custom_call_target="Cholesky" | custom-call | tf_op jit(solution)/shard_map/jit(cholesky)/cholesky | solution.py:41
  147.5 4.6 %fusion.6 = f32[32,16384]{1,0:T(8,128)S(1)} fusion(f32[4,8,128,128]{3,2,1,0:T(8,128)} %bitcast.52, f32[1,32,32]{1,2,0:T(8,128)S(1)} %custom-call.6), kind=kOutput, calls=%fused_computation.13 | convolution fusion | flops 201326592 | bytes 4198400 | tf_op jit(solution)/shard_map/triangular_solve/dot.1 | solution.py:31
  154.2 12.4 %all_to_all.10 = f32[32,1,1024]{2,1,0:T(1,128)S(1)} all-to-all(f32[32,1,1024]{2,1,0:T(1,128)S(1)} %reshape.39), channel_id=1, replica_groups=mesh['gx'=32,'gy'=16] {'gx'}, dimensions={0} | all-to-all | bytes 262144 | tf_op jit(solution)/shard_map/all_to_all | solution.py:46
  167.9 2.9 %cholesky.96 = f32[32,32]{1,0:T(8,128)S(1)} custom-call(f32[32,32]{1,0:T(8,128)S(1)} %fusion.25), custom_call_target="Cholesky" | custom-call | tf_op jit(solution)/shard_map/jit(cholesky)/cholesky | solution.py:48
  172.1 16.8 %all-gather.1 = f32[512,32]{1,0:T(8,128)S(1)} all-gather(f32[32,32]{1,0:T(8,128)S(1)} %fusion.29), channel_id=3, replica_groups=mesh['gx'=32,'gy'=16] {'gy'}, dimensions={0}, use_global_device_ids=true | all-gather | bytes 69632 | tf_op jit(solution)/shard_map/all_gather | solution.py:49
  189.4 2.9 %cholesky.107 = f32[32,32]{1,0:T(8,128)S(1)} custom-call(f32[32,32]{1,0:T(8,128)S(1)} %fusion.24), custom_call_target="Cholesky" | custom-call | tf_op jit(solution)/shard_map/jit(cholesky)/cholesky | solution.py:41
  (73 shorter events, 47.7 us)
Async XLA Ops:
  0.0 9.3 %copy-start.3 = (f32[32,8,16,128]{3,2,1,0:T(8,128)S(1)}, f32[32,8,16,128]{3,2,1,0:T(8,128)}, u32[]{:S(2)}) copy-start(f32[32,8,16,128]{3,2,1,0:T(8,128)} %param.5) | copy-start | bytes 6291460
  2.6 1.3 copy-start.2
  4.0 9.9 %collective-permute-start.1 = (f32[32,8,1,128]{3,1,2,0:T(8,128)S(1)}, f32[32,8,1,128]{3,1,2,0:T(8,128)S(1)}, u32[]{:S(2)}, u32[]{:S(2)}) collective-permute-start(f32[32,8,1,128]{3,1,2,0:T(8,128)S(1)} %get-tuple-element.13), channel_id=1, source_target_pairs={{0,16},{16,32},{32,48},{48,64},{64,80},{80,96},{96,112},{112,128},... | collective-permute-start | bytes 393224 | tf_op jit(solution)/shard_map/ppermute | solution.py:13
  8.0 6.1 %collective-permute-start = (f32[32,8,1,128]{3,1,2,0:T(8,128)S(1)}, f32[32,8,1,128]{3,1,2,0:T(8,128)S(1)}, u32[]{:S(2)}, u32[]{:S(2)}) collective-permute-start(f32[32,8,1,128]{3,1,2,0:T(8,128)S(1)} %get-tuple-element.14), channel_id=1, source_target_pairs={{16,0},{32,16},{48,32},{64,48},{80,64},{96,80},{112,96},{128,112},... | collective-permute-start | bytes 393224 | tf_op jit(solution)/shard_map/ppermute | solution.py:16
  14.4 16.3 %copy-start.4 = (f32[8,16,128]{2,1,0:T(8,128)S(1)}, f32[8,16,128]{2,1,0:T(8,128)}, u32[]{:S(2)}) copy-start(f32[8,16,128]{2,1,0:T(8,128)} %param.6) | copy-start | bytes 196612
  18.3 3.6 %copy-start = (f32[32,8,18,128]{0,1,3,2:T(8,128)}, f32[32,8,18,128]{0,1,3,2:T(8,128)S(1)}, u32[]{:S(2)}) copy-start(f32[32,8,18,128]{0,1,3,2:T(8,128)S(1)} %pad_maximum_fusion) | copy-start | bytes 7077892
  22.0 16.7 %collective-permute-start.2 = (f32[32,8,18,1]{0,1,3,2:T(8,128)S(1)}, f32[32,8,18,1]{0,1,3,2:T(8,128)S(1)}, u32[]{:S(2)}, u32[]{:S(2)}) collective-permute-start(f32[32,8,18,1]{0,1,3,2:T(8,128)S(1)} %get-tuple-element.6), channel_id=1, source_target_pairs={{1,0},{2,1},{3,2},{4,3},{5,4},{6,5},{7,6},{8,7},{9,8},{10,9},{11,1... | collective-permute-start | bytes 55304 | tf_op jit(solution)/shard_map/ppermute | solution.py:16
  28.7 12.3 %collective-permute-start.3 = (f32[32,8,18,1]{0,1,3,2:T(8,128)S(1)}, f32[32,8,18,1]{0,1,3,2:T(8,128)S(1)}, u32[]{:S(2)}, u32[]{:S(2)}) collective-permute-start(f32[32,8,18,1]{0,1,3,2:T(8,128)S(1)} %get-tuple-element.8), channel_id=1, source_target_pairs={{0,1},{1,2},{2,3},{3,4},{4,5},{5,6},{6,7},{7,8},{8,9},{9,10},{10,1... | collective-permute-start | bytes 55304 | tf_op jit(solution)/shard_map/ppermute | solution.py:13
  51.4 6.8 %collective-permute-start.4 = (f32[32,8,1,128]{3,1,2,0:T(8,128)S(1)}, f32[32,8,1,128]{3,1,2,0:T(8,128)S(1)}, u32[]{:S(2)}, u32[]{:S(2)}) collective-permute-start(f32[32,8,1,128]{3,1,2,0:T(8,128)S(1)} %get-tuple-element.12), channel_id=1, source_target_pairs={{16,0},{32,16},{48,32},{64,48},{80,64},{96,80},{112,96},{128,112},... | collective-permute-start | bytes 393224 | tf_op jit(solution)/shard_map/ppermute | solution.py:16
  52.7 6.4 %collective-permute-start.5 = (f32[32,8,1,128]{3,1,2,0:T(8,128)S(1)}, f32[32,8,1,128]{3,1,2,0:T(8,128)S(1)}, u32[]{:S(2)}, u32[]{:S(2)}) collective-permute-start(f32[32,8,1,128]{3,1,2,0:T(8,128)S(1)} %get-tuple-element.11), channel_id=1, source_target_pairs={{0,16},{16,32},{32,48},{48,64},{64,80},{80,96},{96,112},{112,128},... | collective-permute-start | bytes 393224 | tf_op jit(solution)/shard_map/ppermute | solution.py:13
  64.7 8.3 %collective-permute-start.6 = (f32[32,8,18,1]{0,1,3,2:T(8,128)S(1)}, f32[32,8,18,1]{0,1,3,2:T(8,128)S(1)}, u32[]{:S(2)}, u32[]{:S(2)}) collective-permute-start(f32[32,8,18,1]{0,1,3,2:T(8,128)S(1)} %copy.107), channel_id=1, source_target_pairs={{1,0},{2,1},{3,2},{4,3},{5,4},{6,5},{7,6},{8,7},{9,8},{10,9},{11,1... | collective-permute-start | bytes 55304 | tf_op jit(solution)/shard_map/ppermute | solution.py:16
  70.7 4.7 %collective-permute-start.7 = (f32[32,8,18,1]{0,1,3,2:T(8,128)S(1)}, f32[32,8,18,1]{0,1,3,2:T(8,128)S(1)}, u32[]{:S(2)}, u32[]{:S(2)}) collective-permute-start(f32[32,8,18,1]{0,1,3,2:T(8,128)S(1)} %copy.108), channel_id=1, source_target_pairs={{0,1},{1,2},{2,3},{3,4},{4,5},{5,6},{6,7},{7,8},{8,9},{9,10},{10,1... | collective-permute-start | bytes 55304 | tf_op jit(solution)/shard_map/ppermute | solution.py:13
  81.8 1.3 copy-start.1
  86.9 23.1 %all-to-all-start = ((f32[32,1,1024]{2,1,0:T(1,128)}), f32[32,1,1024]{2,1,0:T(1,128)S(1)}, u32[]{:S(2)}, u32[]{:S(2)}) async-start(f32[32,1,1024]{2,1,0:T(1,128)} %reshape.37), calls=%async_computation | async-start | bytes 262144 | tf_op jit(solution)/shard_map/all_to_all | solution.py:46
